TPU v7x, 32 devices: a whole 2x2x4 slice. The times are simulated.
32 devices in a mesh: rep: 16 (over z, y, core), zero: 2 (over x).
Axes of the slice: x: 2, y: 2, z: 4, core: 2. Of those that a mesh axis runs over, the one named last changes fastest.
Arguments:
- tokens: bfloat16 [8192, 1536], P(('rep', 'zero')), may hold values from -6 to 6
- cotangent: bfloat16 [8192, 1536], P(('rep', 'zero')), may hold values from -6 to 6
- segment_ids: int32 [8192], P(('rep', 'zero')), may hold values from 0 to 52, never falling along the last dimension, each value on 1 to 512 neighbouring positions
- master: float32 [14647296], P('zero')
- first_moment: float32 [14647296], P('zero')
- second_moment: float32 [14647296], P('zero')
- step_count: int32 [], replicated, may hold values from 1 to 20
- rates: float32 [2, 9], replicated, may hold values from 0 to 1
Outputs:
- mixed: bfloat16 [8192, 1536], P(('rep', 'zero'))
- input_grad: bfloat16 [8192, 1536], P(('rep', 'zero'))
- new_first: float32 [14647296], P('zero')
- new_second: float32 [14647296], P('zero')
- new_master: float32 [14647296], P('zero')
Inputs may be any that keep to these rules, and one draw needn't show every extreme that they name: `segment_ids`: ids never fall along the tokens; a document is a run of equal ids of at most 512 tokens.
All inputs are finite; a program needn't handle non-finite values.
Results may differ from a plain program's by a relative error of at most 0.012.
Values may be sent and summed in bfloat16 or wider, within the bound.
No kernel may reach another device: no remote copies, remote signals or barrier semaphores. Data moves between devices by JAX's collectives and lax.ppermute only.
A program may use at most 512 MiB of HBM per device.

v0:
```python
import functools
import jax
import jax.numpy as jnp
from jax import lax
from jax.sharding import PartitionSpec as P

D = 1536
DI = 3072
NS = 128
HD = 64
NH = 48
E = 6448
CONV = 3328
EPSILON = 1e-05
ADAM_EPSILON = 1e-08
BETA_ONE = 0.5
BETA_TWO = 0.5
HEAD_GROUP = 4
HIGHEST = lax.Precision.HIGHEST


def piece_bounds():
    amounts = [D * E, DI * D, 4 * CONV, CONV, D, DI, NH, NH, NH]
    bounds = [0]
    for amount in amounts:
        bounds.append(bounds[-1] + amount)
    return bounds


def unpack(flat_values):
    bounds = piece_bounds()
    shapes = [(D, E), (DI, D), (4, CONV), (CONV,), (D,), (DI,), (NH,), (NH,), (NH,)]
    return tuple(
        (
            flat_values[bounds[piece_index] : bounds[piece_index + 1]].reshape(shapes[piece_index])
            for piece_index in range(9)
        )
    )


def contract(left, right, left_dim, right_dim):
    return lax.dot_general(
        left, right, (((left_dim,), (right_dim,)), ((), ())), preferred_element_type=jnp.float32
    )


def prenorm(residual, norm_gain):
    inverse_rms = lax.rsqrt(jnp.mean(residual * residual, axis=-1, keepdims=True) + EPSILON)
    return residual * inverse_rms * norm_gain


def head_group(contact, allowed, inputs):
    group_decay, group_step, group_values = inputs
    log_gap = group_decay[:, :, None] - group_decay[:, None, :]
    kernel = (
        jnp.exp(jnp.where(allowed[None], log_gap, -1e30)) * contact[None] * group_step[:, None, :]
    )
    return jnp.einsum("gts,gsp->gtp", kernel, group_values, precision=HIGHEST)


def mixer(
    segment_ids, projected, filter_taps, filter_bias, step_bias, log_decay, skip_weight, gate_gain
):
    length = projected.shape[0]
    gate_raw = projected[:, :DI]
    filter_in = projected[:, DI : DI + CONV]
    step_raw = projected[:, DI + CONV :]
    padded = jnp.pad(filter_in, ((3, 0), (0, 0)))
    padded_ids = jnp.pad(segment_ids, (3, 0), constant_values=-1)
    filtered = jnp.zeros_like(filter_in) + filter_bias[None, :]
    for offset in range(4):
        same_segment = (padded_ids[offset : offset + length] == segment_ids)[:, None]
        filtered = filtered + jnp.where(
            same_segment, padded[offset : offset + length] * filter_taps[offset][None, :], 0.0
        )
    activated = jax.nn.silu(filtered)
    values = activated[:, :DI].reshape(length, NH, HD)
    b_input = activated[:, DI : DI + NS]
    c_output = activated[:, DI + NS :]
    step_size = jax.nn.softplus(step_raw + step_bias[None, :])
    cumulative = jnp.cumsum(step_size * (-jnp.exp(log_decay))[None, :], axis=0)
    row_index = lax.broadcasted_iota(jnp.int32, (length, length), 0)
    col_index = lax.broadcasted_iota(jnp.int32, (length, length), 1)
    allowed = (col_index <= row_index) & (segment_ids[:, None] == segment_ids[None, :])
    contact = lax.dot_general(c_output, b_input, (((1,), (1,)), ((), ())), precision=HIGHEST)
    groups = NH // HEAD_GROUP
    grouped_decay = cumulative.T.reshape(groups, HEAD_GROUP, length)
    grouped_step = step_size.T.reshape(groups, HEAD_GROUP, length)
    grouped_values = values.transpose(1, 0, 2).reshape(groups, HEAD_GROUP, length, HD)
    scanned = lax.map(
        jax.checkpoint(functools.partial(head_group, contact, allowed)),
        (grouped_decay, grouped_step, grouped_values),
    )
    ssd_out = (
        scanned.reshape(NH, length, HD).transpose(1, 0, 2) + skip_weight[None, :, None] * values
    )
    gated = ssd_out.reshape(length, DI) * jax.nn.silu(gate_raw)
    inverse_rms = lax.rsqrt(jnp.mean(gated * gated, axis=-1, keepdims=True) + EPSILON)
    return gated * inverse_rms * gate_gain


def adamw(gradient, first_moment, second_moment, weights, start, step_count, rates):
    position = start + lax.iota(jnp.int32, gradient.shape[0])
    bounds = piece_bounds()
    learn_rate = jnp.zeros_like(gradient)
    decay_rate = jnp.zeros_like(gradient)
    for piece_index in range(9):
        inside = (position >= bounds[piece_index]) & (position < bounds[piece_index + 1])
        learn_rate = learn_rate + jnp.where(inside, rates[0, piece_index], 0.0)
        decay_rate = decay_rate + jnp.where(inside, rates[1, piece_index], 0.0)
    new_first = BETA_ONE * first_moment + (1.0 - BETA_ONE) * gradient
    new_second = BETA_TWO * second_moment + (1.0 - BETA_TWO) * gradient * gradient
    power = step_count.astype(gradient.dtype)
    correct_one = 1.0 - jnp.power(BETA_ONE, power)
    correct_two = 1.0 - jnp.power(BETA_TWO, power)
    update = (
        new_first / correct_one / (jnp.sqrt(new_second / correct_two) + ADAM_EPSILON)
        + decay_rate * weights
    )
    return (new_first, new_second, weights - learn_rate * update)


def gather_weights(master):
    rep_size = lax.axis_size("rep")
    zero_size = lax.axis_size("zero")
    shard_size = master.shape[0]
    piece_size = shard_size // rep_size
    rep_index = lax.axis_index("rep")
    zero_index = lax.axis_index("zero")
    own = master.astype(jnp.bfloat16)
    mine = lax.dynamic_slice_in_dim(own, rep_index * piece_size, piece_size)
    if zero_size == 2:
        other_piece = lax.ppermute(mine, "zero", [(0, 1), (1, 0)])
        other = lax.all_gather(other_piece, "rep", axis=0, tiled=True)
        shards = [jnp.where(zero_index == 0, own, other), jnp.where(zero_index == 0, other, own)]
    else:
        across = lax.all_gather(mine, "zero", axis=0, tiled=True)
        shards = [
            lax.all_gather(
                lax.dynamic_slice_in_dim(across, shard * piece_size, piece_size),
                "rep",
                axis=0,
                tiled=True,
            )
            for shard in range(zero_size)
        ]
    return jnp.concatenate(shards)


def reduce_gradient(pieces, shard_size):
    zero_size = lax.axis_size("zero")
    total_params = shard_size * zero_size
    flat_grad = jnp.zeros((total_params,), jnp.bfloat16)
    offset = 0
    for piece_grad in pieces:
        flat_piece = piece_grad.reshape(-1).astype(jnp.bfloat16)
        flat_grad = lax.dynamic_update_slice_in_dim(flat_grad, flat_piece, offset, 0)
        offset += flat_piece.shape[0]
    summed = lax.psum(flat_grad, ("rep", "zero"))
    return lax.dynamic_slice_in_dim(summed, lax.axis_index("zero") * shard_size, shard_size)


def body(tokens, cotangent, segment_ids, master, first_moment, second_moment, step_count, rates):
    gathered = gather_weights(master)
    (
        in_projection,
        out_projection,
        filter_taps,
        filter_bias,
        norm_gain,
        gate_gain,
        step_bias,
        log_decay,
        skip_weight,
    ) = unpack(gathered)
    residual = tokens.astype(jnp.float32)
    normed, norm_pullback = jax.vjp(prenorm, residual, norm_gain.astype(jnp.float32))
    normed_low = normed.astype(jnp.bfloat16)
    projected = jnp.dot(normed_low, in_projection, preferred_element_type=jnp.float32)
    mixer_out, mixer_pullback = jax.vjp(
        functools.partial(mixer, segment_ids),
        projected,
        filter_taps.astype(jnp.float32),
        filter_bias.astype(jnp.float32),
        step_bias.astype(jnp.float32),
        log_decay.astype(jnp.float32),
        skip_weight.astype(jnp.float32),
        gate_gain.astype(jnp.float32),
    )
    mixer_low = mixer_out.astype(jnp.bfloat16)
    branch = jnp.dot(mixer_low, out_projection, preferred_element_type=jnp.float32)
    mixed = (residual + branch).astype(jnp.bfloat16)
    grad_out = contract(mixer_low, cotangent, 0, 0)
    grad_mixer = contract(cotangent, out_projection, 1, 1)
    grad_projected, grad_taps, grad_bias, grad_step_bias, grad_decay, grad_skip, grad_gate_gain = (
        mixer_pullback(grad_mixer)
    )
    projected_low = grad_projected.astype(jnp.bfloat16)
    grad_in = contract(normed_low, projected_low, 0, 0)
    grad_normed = contract(projected_low, in_projection, 1, 1)
    grad_residual, grad_norm_gain = norm_pullback(grad_normed)
    input_grad = (cotangent.astype(jnp.float32) + grad_residual).astype(jnp.bfloat16)
    pieces = [
        grad_in,
        grad_out,
        grad_taps,
        grad_bias,
        grad_norm_gain,
        grad_gate_gain,
        grad_step_bias,
        grad_decay,
        grad_skip,
    ]
    shard_size = master.shape[0]
    gradient = reduce_gradient(pieces, shard_size).astype(jnp.float32)
    shard_start = lax.axis_index("zero") * shard_size
    new_first, new_second, new_master = adamw(
        gradient, first_moment, second_moment, master, shard_start, step_count, rates
    )
    return (mixed, input_grad, new_first, new_second, new_master)


def solution(mesh):
    in_specs = (
        P(("rep", "zero"), None),
        P(("rep", "zero"), None),
        P(("rep", "zero")),
        P("zero"),
        P("zero"),
        P("zero"),
        P(),
        P(),
    )
    out_specs = (
        P(("rep", "zero"), None),
        P(("rep", "zero"), None),
        P("zero"),
        P("zero"),
        P("zero"),
    )
    return jax.shard_map(body, mesh=mesh, in_specs=in_specs, out_specs=out_specs, check_vma=False)
```

profile of v0, /device:TPU:0, one launch (start us, length us, event | category | flops | bytes accessed | tf_op | source)
XLA Modules:
  0.0 1149.5 jit_solution(654857939169219657)
XLA Ops:
  7.2 16.2 %convert_element_type.91 = bf16[7323648]{0:T(1024)(128)(2,1)} convert(f32[7323648]{0:T(1024)} %param.15) | non-fusion elementwise | flops 7323648 | bytes 43941888 | tf_op jit(solution)/shard_map/convert_element_type | solution.py:130
  24.7 3.0 collective-permute-start
  27.7 20.3 %collective-permute-done = bf16[457728]{0:T(1024)(128)(2,1)S(1)} collective-permute-done((bf16[457728]{0:T(1024)(128)(2,1)S(1)}, bf16[457728]{0:T(1024)(128)(2,1)S(1)}, u32[]{:S(2)}, u32[]{:S(2)}) %collective-permute-start) | collective-permute-done | bytes 915488 | tf_op jit(solution)/shard_map/ppermute | solution.py:133
  50.1 113.6 %all-gather.2.cloned.1.call-done = bf16[7323648]{0:T(1024)(128)(2,1)} async-done(((bf16[457728]{0:T(1024)(128)(2,1)}), bf16[7323648]{0:T(1024)(128)(2,1)}) %all-gather.2.cloned.1.call-update) | async-done | bytes 14647312 | tf_op jit(solution)/shard_map/all_gather | solution.py:134
  163.8 25.1 %broadcast_select_fusion = (bf16[7323648]{0:T(1024)(128)(2,1)}, bf16[7323648]{0:T(1024)(128)(2,1)}) fusion(bf16[7323648]{0:T(1024)(128)(2,1)} %all-gather.2.cloned.1.call-done, pred[]{:T(512)S(6)} %eq.39, f32[7323648]{0:T(1024)} %param.15), kind=kLoop, calls=%fused_computation.81 | loop fusion | flops 21970944 | bytes 73236480 | tf_op jit(solution)/shard_map/jit(_where)/select_n | solution.py:135
  194.4 20.2 %pad_maximum_fusion = bf16[9904128]{0:T(1024)(128)(2,1)} fusion(bf16[7323648]{0:T(1024)(128)(2,1)} %get-tuple-element.429, bf16[7323648]{0:T(1024)(128)(2,1)} %get-tuple-element.428), kind=kLoop, calls=%fused_computation.80 | loop fusion | flops 39616512 | bytes 49102848 | tf_op jit(solution)/shard_map/concatenate | solution.py:147
  214.6 32.9 %reshape.260 = bf16[1536,6448]{1,0:T(8,128)(2,1)} reshape(bf16[9904128]{0:T(1024)(128)(2,1)} %pad_maximum_fusion) | data formatting | bytes 39616512 | tf_op jit(solution)/shard_map/reshape | solution.py:35
  247.5 13.0 %fusion.80 = f32[256,6448]{0,1:T(8,128)S(1)} fusion(bf16[1536,6448]{1,0:T(8,128)(2,1)} %reshape.260, bf16[256,1536]{1,0:T(8,128)(2,1)} %param.12, f32[1536]{0:T(1024)S(1)} %slice_convert_fusion.3, f32[256]{0:T(256)S(1)} %fusion.99), kind=kOutput, calls=%fused_computation.139 | convolution fusion | flops 5072486400 | bytes 27204608 | tf_op jit(solution)/shard_map/dot_general | solution.py:179
  260.8 7.5 fusion.64
  271.7 9.1 slice.224
  282.3 30.5 %while.33 = (s32[]{:T(128)}, f32[12,4,256,64]{2,3,1,0:T(8,128)S(1)}, f32[12,4,256]{2,1,0:T(4,128)S(1)}, f32[1,256,256]{2,1,0:T(8,128)}, f32[12,4,256]{2,1,0:T(4,...) while((s32[]{:T(128)}, f32[12,4,256,64]{2,3,1,0:T(8,128)S(1)}, ...), condition=%wide.region_4.5_spmd.clone, body=%wide.region_3.4_spmd.clone.sunk | while | flops 202375168 | bytes 881761 | solution.py:90
  315.5 4.1 multiply_reduce_fusion.9
  319.6 18.0 %slice.185 = bf16[3072,1536]{1,0:T(8,128)(2,1)} reshape(bf16[4718592]{0:T(1024)(128)(2,1)} %slice.224) | data formatting | bytes 18874368 | tf_op jit(solution)/shard_map/slice | solution.py:35
  337.6 6.8 convolution_convert_fusion.1
  344.4 3.8 multiply_reduce_fusion.7
  348.2 6.7 multiply_reduce_fusion.6
  357.0 78.3 %while.34 = (s32[]{:T(128)}, f32[256,256]{1,0:T(8,128)S(1)}, f32[12,4,256]{2,1,0:T(4,128)S(1)}, f32[12,4,256]{2,1,0:T(4,128)S(1)}, f32[12,4,256,64]{2,3,1,0:T(8,...) while((s32[]{:T(128)}, f32[256,256]{1,0:T(8,128)S(1)}, ...), condition=%wide.region_12.13_spmd.clone, body=%wide.region_7.12_spmd.clone.sunk | while | flops 407370752 | bytes 4986067 | solution.py:90
  443.1 5.0 bitcast_add_fusion
  449.0 8.4 multiply_reduce_fusion.4
  457.5 3.6 broadcast_multiply_fusion
  462.1 6.8 pad_add_fusion
  468.9 13.1 %fusion.72 = (bf16[1536]{0:T(1024)(128)(2,1)S(1)}, f32[256]{0:T(256)S(1)}, f32[256,1536]{1,0:T(8,128)}) fusion(bf16[256,1536]{1,0:T(8,128)(2,1)} %param.12, f32[256]{0:T(256)S(1)} %copy-done.46, f32[1536]{0:T(1024)S(1)} %slice_convert_fusion.3, bf16[1536,6448]{1,0:T(8,128)(2,1)} %reshape.260, f32[256,3072]{0,1:T(8,128)} %get-tuple-element.432, ...), kind=kOutput, calls=%fused_computation.131 | convolution fusion | flops 5078616064 | bytes 28781568 | tf_op jit(solution)/shard_map/dot_general | solution.py:42
  482.0 13.1 %convolution_convert_fusion = bf16[1536,6448]{0,1:T(8,128)(2,1)} fusion(bf16[256,1536]{1,0:T(8,128)(2,1)} %param.12, f32[1536]{0:T(1024)S(1)} %slice_convert_fusion.3, f32[256]{0:T(256)S(1)} %copy-done.46, f32[256,3072]{0,1:T(8,128)} %get-tuple-element.432, f32[256,3328]{0,1:T(8,128)} %pad_add_fusion, f32[256,48]{0,1:T(8,128)S(1)} %get-tuple-element.416), kind=kOutput, calls=%fused_computation.79 | convolution fusion | flops 5087342592 | bytes 27204608 | tf_op jit(solution)/shard_map/dot_general | solution.py:42
  495.1 18.1 %convert_element_type.108 = bf16[4718592]{0:T(1024)(128)(2,1)} reshape(bf16[3072,1536]{1,0:T(8,128)(2,1)} %convolution_convert_fusion.1) | data formatting | bytes 18874368 | tf_op jit(solution)/shard_map/convert_element_type | solution.py:156
  514.3 25.0 %copy.38 = bf16[1536,6448]{1,0:T(8,128)(2,1)} copy(bf16[1536,6448]{0,1:T(8,128)(2,1)} %convolution_convert_fusion) | data formatting | bytes 39616512 | tf_op jit(solution)/shard_map/convert_element_type | solution.py:156
  539.3 36.0 %convert_element_type.106 = bf16[9904128]{0:T(1024)(128)(2,1)} reshape(bf16[1536,6448]{1,0:T(8,128)(2,1)} %copy.38) | data formatting | bytes 39616512 | tf_op jit(solution)/shard_map/convert_element_type | solution.py:156
  575.4 16.7 %dynamic_update_slice.61 = bf16[14647296]{0:T(1024)(128)(2,1)} pad(bf16[9904128]{0:T(1024)(128)(2,1)} %convert_element_type.106, bf16[]{:T(256)} %constant.161.clone.1), padding=0_4743168 | pad | bytes 49102848 | tf_op jit(solution)/shard_map/dynamic_update_slice | solution.py:157
  592.1 8.7 constant_dynamic-update-slice_fusion.1
  611.7 3.3 fusion.74
  614.9 7.4 fusion.68
  622.3 430.1 %all-reduce.19.cloned.1.call-done = bf16[14647296]{0:T(1024)(128)(2,1)} async-done(((bf16[14647296]{0:T(1024)(128)(2,1)}), bf16[14647296]{0:T(1024)(128)(2,1)}) %all-reduce.19.cloned.1.call-update) | async-done | bytes 29294608 | tf_op jit(solution)/shard_map/psum | solution.py:159
  1052.5 90.0 %multiply_subtract_fusion = (f32[7323648]{0:T(1024)}, f32[7323648]{0:T(1024)}, f32[7323648]{0:T(1024)}) fusion(f32[7323648]{0:T(1024)} %param.15, f32[]{:T(128)} %bitcast.37, f32[]{:T(128)} %bitcast.36, f32[]{:T(128)} %bitcast.35, f32[]{:T(128)} %bitcast.34, f32[]{:T(128)} %bitcast.33, f32[]{:T(128)} %bitcast.32, f32[]{:T(128)} %bitcast.31, f32[]{:T(128)} %bitcast.30, ...), kind=kLoop, calls=%fused_computation.50 | loop fusion | flops 563920896 | bytes 190414928 | tf_op jit(solution)/shard_map/sub | solution.py:120
  (307 shorter events, 147.2 us)
Async XLA Ops:
  7.2 156.6 %all-gather.2.cloned.1.call-start = ((), (), s32[]{:S(2)}) async-start(), calls=%async_computation | async-start | bytes 15562752 | tf_op jit(solution)/shard_map/all_gather | solution.py:134
  7.2 41.8 %copy-start.10 = (bf16[256,1536]{1,0:T(8,128)(2,1)S(1)}, bf16[256,1536]{1,0:T(8,128)(2,1)}, u32[]{:S(2)}) copy-start(bf16[256,1536]{1,0:T(8,128)(2,1)} %param.12) | copy-start | bytes 2359300
  23.4 25.9 %copy-start.18 = (s32[256]{0:T(256)S(1)}, s32[256]{0:T(256)}, u32[]{:S(2)}) copy-start(s32[256]{0:T(256)} %param.14) | copy-start | bytes 3076
  24.7 23.3 %collective-permute-start = (bf16[457728]{0:T(1024)(128)(2,1)S(1)}, bf16[457728]{0:T(1024)(128)(2,1)S(1)}, u32[]{:S(2)}, u32[]{:S(2)}) collective-permute-start(bf16[457728]{0:T(1024)(128)(2,1)S(1)} %dynamic_slice.59), channel_id=1, source_target_pairs={{0,1},{1,0},{2,3},{3,2},{4,5},{5,4},{6,7},{7,6},{8,9},{9,8},{10,11... | collective-permute-start | bytes 2746376 | tf_op jit(solution)/shard_map/ppermute | solution.py:133
  49.0 1003.5 %all-reduce.19.cloned.1.call-start = ((), (), s32[]{:S(2)}) async-start(), calls=%async_computation.1 | async-start | bytes 58589184 | tf_op jit(solution)/shard_map/psum | solution.py:159
  49.3 139.5 %copy-start.33 = (f32[256]{0:T(256)}, f32[256]{0:T(256)S(1)}, u32[]{:S(2)}) copy-start(f32[256]{0:T(256)S(1)} %fusion.75) | copy-start | bytes 3076
  49.3 198.2 %copy-start.45 = (f32[256]{0:T(256)}, f32[256]{0:T(256)S(1)}, u32[]{:S(2)}) copy-start(f32[256]{0:T(256)S(1)} %fusion.99) | copy-start | bytes 3076
  49.4 211.4 %copy-start.35 = (pred[256]{0:T(512)(128)(4,1)}, pred[256]{0:T(512)(128)(4,1)S(1)}, u32[]{:S(2)}) copy-start(pred[256]{0:T(512)(128)(4,1)S(1)} %get-tuple-element.462) | copy-start | bytes 772
  49.4 211.4 %copy-start.37 = (pred[256]{0:T(512)(128)(4,1)}, pred[256]{0:T(512)(128)(4,1)S(1)}, u32[]{:S(2)}) copy-start(pred[256]{0:T(512)(128)(4,1)S(1)} %get-tuple-element.463) | copy-start | bytes 772
  49.4 211.4 %copy-start.39 = (pred[256]{0:T(512)(128)(4,1)}, pred[256]{0:T(512)(128)(4,1)S(1)}, u32[]{:S(2)}) copy-start(pred[256]{0:T(512)(128)(4,1)S(1)} %get-tuple-element.464) | copy-start | bytes 772
  194.4 66.4 %copy-start.21 = (f32[3328]{0:T(1024)}, f32[3328]{0:T(1024)S(1)}, u32[]{:S(2)}) copy-start(f32[3328]{0:T(1024)S(1)} %get-tuple-element.440) | copy-start | bytes 39940
  194.4 66.4 %copy-start.23 = (f32[3328]{0:T(1024)}, f32[3328]{0:T(1024)S(1)}, u32[]{:S(2)}) copy-start(f32[3328]{0:T(1024)S(1)} %get-tuple-element.441) | copy-start | bytes 39940
  194.4 66.4 %copy-start.25 = (f32[3328]{0:T(1024)}, f32[3328]{0:T(1024)S(1)}, u32[]{:S(2)}) copy-start(f32[3328]{0:T(1024)S(1)} %get-tuple-element.442) | copy-start | bytes 39940
  194.4 66.4 %copy-start.27 = (f32[3328]{0:T(1024)}, f32[3328]{0:T(1024)S(1)}, u32[]{:S(2)}) copy-start(f32[3328]{0:T(1024)S(1)} %get-tuple-element.443) | copy-start | bytes 39940
  260.5 20.3 %copy-start.7 = (f32[256,6448]{0,1:T(8,128)}, f32[256,6448]{0,1:T(8,128)S(1)}, u32[]{:S(2)}) copy-start(f32[256,6448]{0,1:T(8,128)S(1)} %fusion.80) | copy-start | bytes 19808260
  260.8 7.5 copy-start.3
  271.7 9.1 copy-start.42
  271.7 9.1 copy-start.48
  282.3 30.5 %copy-start.44 = (f32[48]{0:T(128)S(1)}, f32[48]{0:T(128)}, u32[]{:S(2)}) copy-start(f32[48]{0:T(128)} %get-tuple-element.430) | copy-start | bytes 580
  337.6 6.8 copy-start
  337.6 6.8 copy-start.12
  348.2 8.8 copy-start.9
  443.0 5.9 copy-start.15
  449.0 8.4 copy-start.22
  449.0 8.4 copy-start.24
  449.0 8.4 copy-start.26
  449.0 8.4 copy-start.28
  462.1 6.8 copy-start.46
  495.1 18.1 %copy-start.31 = (f32[3072]{0:T(1024)S(1)}, f32[3072]{0:T(1024)}, u32[]{:S(2)}) copy-start(f32[3072]{0:T(1024)} %get-tuple-element.413) | copy-start | bytes 36868
  495.1 19.0 %copy-start.30 = (f32[3328]{0:T(1024)S(1)}, f32[3328]{0:T(1024)}, u32[]{:S(2)}) copy-start(f32[3328]{0:T(1024)} %get-tuple-element.365) | copy-start | bytes 39940
  592.1 9.3 copy-start.32
  592.1 12.2 %copy-start.41 = (bf16[3072]{0:T(1024)(128)(2,1)S(1)}, bf16[3072]{0:T(1024)(128)(2,1)}, u32[]{:S(2)}) copy-start(bf16[3072]{0:T(1024)(128)(2,1)} %get-tuple-element.368) | copy-start | bytes 18436
  (32 other events, 132.9 us)
Sparse Core Ops, SparseCore 0:
  49.1 114.6 all-gather.1
  610.3 442.1 all-reduce.18
where the time goes:
time: 1160 us; the launch traced here: 1150 us
  waiting for transfers between devices  564 us (49%)
  other arithmetic  214 us (18%)
  local copies, waits for them, and re-layouts  206 us (18%)
  matrix products  146 us (13%)
  between operations  15.6 us (1%)
    psum x1, waiting for transfers between devices, reduce_gradient(): summed = lax.psum(flat_grad, ('rep', 'zero'))  430 us
    all_gather x1, waiting for transfers between devices, gather_weights(): other = lax.all_gather(other_piece, 'rep', axis=0, tiled=True)  114 us
    sub x1, other arithmetic, adamw(): return (new_first, new_second, weights - learn_rate * update)  90 us
    dot_general x36, matrix products, head_group(): return jnp.einsum('gts,gsp->gtp', kernel, group_values, precision=HIGHEST)  83.4 us
    convert_element_type x4, local copies, waits for them, and re-layouts, reduce_gradient(): flat_piece = piece_grad.reshape(-1).astype(jnp.bfloat16)  79.2 us
    dot_general x4, matrix products, contract(): lax.dot_general(left, right, (((left_dim,), (right_dim,)), ((), ())), pre...  36.8 us
    dynamic_update_slice x9, local copies, waits for them, and re-layouts, reduce_gradient(): lax.dynamic_update_slice_in_dim(flat_grad, flat_piece, offset, 0)  34.7 us
    reshape x1, local copies, waits for them, and re-layouts, unpack(): flat_values[bounds[piece_index]:bounds[piece_index + 1]]  32.9 us
  transfers between devices with their start and end apart: 3, of which 3 were waited for; matrix products, arithmetic and copies ran while one was open for 1% of the time, Pallas kernels for 0%

commit v1 on v0

--- a/solution.py
+++ b/solution.py
@@ -17,6 +17,25 @@
 BETA_TWO = 0.5
 HEAD_GROUP = 4
 HIGHEST = lax.Precision.HIGHEST
+
+
+def joined_along(tiles, dim):
+    tiles = jnp.moveaxis(tiles, 0, dim)
+    shape = tiles.shape
+    return tiles.reshape(*shape[:dim], shape[dim] * shape[dim + 1], *shape[dim + 2 :])
+
+
+def doubled(shard, axis):
+    devices, index = (lax.axis_size(axis), lax.axis_index(axis))
+    tiles, bit = (shard[None], 1)
+    while bit < devices:
+        partner_block = lax.ppermute(tiles, axis, [(i, i ^ bit) for i in range(devices)])
+        low = index & bit == 0
+        tiles = jnp.concatenate(
+            [jnp.where(low, tiles, partner_block), jnp.where(low, partner_block, tiles)]
+        )
+        bit *= 2
+    return tiles
 
 
 def piece_bounds():
@@ -131,7 +150,7 @@
     mine = lax.dynamic_slice_in_dim(own, rep_index * piece_size, piece_size)
     if zero_size == 2:
         other_piece = lax.ppermute(mine, "zero", [(0, 1), (1, 0)])
-        other = lax.all_gather(other_piece, "rep", axis=0, tiled=True)
+        other = joined_along(doubled(other_piece, "rep"), 0)
         shards = [jnp.where(zero_index == 0, own, other), jnp.where(zero_index == 0, other, own)]
     else:
         across = lax.all_gather(mine, "zero", axis=0, tiled=True)

time: 1160 us -> 1560 us (1.34)
  waiting for transfers between devices: 564 us -> 888 us
  other arithmetic: 214 us -> 263 us
  local copies, waits for them, and re-layouts: 206 us -> 225 us
    ppermute x0 -> x4, waiting for transfers between devices: none -> 436 us  [doubled(): lax.ppermute(tiles, axis, [(i, i ^ bit) for i in range(devices)])]
    all_gather x1 -> x0, waiting for transfers between devices: 114 us -> none  [gather_weights(): other = lax.all_gather(other_piece, 'rep', axis=0, tiled=True)]
    select_n x0 -> x4, other arithmetic: none -> 32.6 us  [doubled(): jnp.where(low, tiles, partner_block)]
  transfers between devices with their start and end apart: 3 -> 6, of which waited for: 3 -> 6; matrix products, arithmetic and copies ran while one was open for 1% -> 1% of each run, Pallas kernels for 0% -> 0%
where the time goes in v1:
time: 1560 us; the launch traced here: 1550 us
  waiting for transfers between devices  888 us (57%)
  other arithmetic  263 us (17%)
  local copies, waits for them, and re-layouts  225 us (14%)
  matrix products  147 us (9%)
  between operations  15.9 us (1%)
    ppermute x4, waiting for transfers between devices, doubled(): lax.ppermute(tiles, axis, [(i, i ^ bit) for i in range(devices)])  436 us
    psum x1, waiting for transfers between devices, reduce_gradient(): summed = lax.psum(flat_grad, ('rep', 'zero'))  432 us
    sub x1, other arithmetic, adamw(): return (new_first, new_second, weights - learn_rate * update)  90.1 us
    dot_general x36, matrix products, head_group(): return jnp.einsum('gts,gsp->gtp', kernel, group_values, precision=HIGHEST)  83.4 us
    convert_element_type x4, local copies, waits for them, and re-layouts, reduce_gradient(): flat_piece = piece_grad.reshape(-1).astype(jnp.bfloat16)  79.2 us
    dot_general x4, matrix products, contract(): lax.dot_general(left, right, (((left_dim,), (right_dim,)), ((), ())), pre...  36.6 us
    dynamic_update_slice x9, local copies, waits for them, and re-layouts, reduce_gradient(): lax.dynamic_update_slice_in_dim(flat_grad, flat_piece, offset, 0)  34.8 us
    reshape x1, local copies, waits for them, and re-layouts, unpack(): flat_values[bounds[piece_index]:bounds[piece_index + 1]]  32.9 us
  transfers between devices with their start and end apart: 6, of which 6 were waited for; matrix products, arithmetic and copies ran while one was open for 1% of the time, Pallas kernels for 0%

profile of v1, /device:TPU:0, one launch (start us, length us, event | category | flops | bytes accessed | tf_op | source)
XLA Modules:
  0.0 1548.4 jit_solution(8972436671228793265)
XLA Ops:
  7.2 16.1 %convert_element_type.91 = bf16[7323648]{0:T(1024)(128)(2,1)} convert(f32[7323648]{0:T(1024)} %param.15) | non-fusion elementwise | flops 7323648 | bytes 43941888 | tf_op jit(solution)/shard_map/convert_element_type | solution.py:149
  27.6 20.3 %collective-permute-done = bf16[457728]{0:T(1024)(128)(2,1)S(1)} collective-permute-done((bf16[457728]{0:T(1024)(128)(2,1)S(1)}, bf16[457728]{0:T(1024)(128)(2,1)S(1)}, u32[]{:S(2)}, u32[]{:S(2)}) %collective-permute-start) | collective-permute-done | bytes 915488 | tf_op jit(solution)/shard_map/ppermute | solution.py:152
  47.9 11.2 broadcast_in_dim.226
  63.1 10.4 broadcast_select_fusion.5
  80.8 40.3 %collective-permute-done.2 = bf16[2,457728]{1,0:T(2,128)(2,1)} collective-permute-done((bf16[2,457728]{1,0:T(2,128)(2,1)S(1)}, bf16[2,457728]{1,0:T(2,128)(2,1)}, u32[]{:S(2)}, u32[]{:S(2)}) %collective-permute-start.2) | collective-permute-done | bytes 1830944 | tf_op jit(solution)/shard_map/ppermute | solution.py:32
  121.1 7.0 broadcast_select_fusion.7
  134.7 78.9 %collective-permute-done.3 = bf16[4,457728]{1,0:T(4,128)(2,1)} collective-permute-done((bf16[4,457728]{1,0:T(4,128)(2,1)}, bf16[4,457728]{1,0:T(4,128)(2,1)}, u32[]{:S(2)}, u32[]{:S(2)}) %collective-permute-start.3) | collective-permute-done | bytes 3661856 | tf_op jit(solution)/shard_map/ppermute | solution.py:32
  213.7 7.1 broadcast_select_fusion.9
  230.6 312.4 %collective-permute-done.4 = bf16[8,457728]{1,0:T(8,128)(2,1)} collective-permute-done((bf16[8,457728]{1,0:T(8,128)(2,1)}, bf16[8,457728]{1,0:T(8,128)(2,1)}, u32[]{:S(2)}, u32[]{:S(2)}) %collective-permute-start.4) | collective-permute-done | bytes 7323680 | tf_op jit(solution)/shard_map/ppermute | solution.py:32
  543.0 8.1 broadcast_select_fusion.3
  552.2 7.1 copy.36
  559.3 25.1 %broadcast_select_fusion = (bf16[7323648]{0:T(1024)(128)(2,1)}, bf16[7323648]{0:T(1024)(128)(2,1)}) fusion(bf16[7323648]{0:T(1024)(128)(2,1)} %bitcast.152, pred[]{:T(512)S(6)} %eq.51, f32[7323648]{0:T(1024)} %param.15), kind=kLoop, calls=%fused_computation.82 | loop fusion | flops 21970944 | bytes 73236480 | tf_op jit(solution)/shard_map/jit(_where)/select_n | solution.py:154
  589.9 20.2 %pad_maximum_fusion = bf16[9904128]{0:T(1024)(128)(2,1)} fusion(bf16[7323648]{0:T(1024)(128)(2,1)} %get-tuple-element.429, bf16[7323648]{0:T(1024)(128)(2,1)} %get-tuple-element.428), kind=kLoop, calls=%fused_computation.80 | loop fusion | flops 39616512 | bytes 49102848 | tf_op jit(solution)/shard_map/concatenate | solution.py:166
  610.1 32.9 %reshape.264 = bf16[1536,6448]{1,0:T(8,128)(2,1)} reshape(bf16[9904128]{0:T(1024)(128)(2,1)} %pad_maximum_fusion) | data formatting | bytes 39616512 | tf_op jit(solution)/shard_map/reshape | solution.py:54
  643.0 13.0 fusion.80
  656.3 7.8 fusion.64
  667.6 9.1 slice.224
  678.2 30.3 %while.33 = (s32[]{:T(128)}, f32[12,4,256,64]{2,3,1,0:T(8,128)S(1)}, f32[12,4,256]{2,1,0:T(4,128)S(1)}, f32[1,256,256]{2,1,0:T(8,128)}, f32[12,4,256]{2,1,0:T(4,...) while((s32[]{:T(128)}, f32[12,4,256,64]{2,3,1,0:T(8,128)S(1)}, ...), condition=%wide.region_4.5_spmd.clone, body=%wide.region_3.4_spmd.clone.sunk | while | flops 202375168 | bytes 881761 | solution.py:109
  715.4 17.9 %slice.185 = bf16[3072,1536]{1,0:T(8,128)(2,1)} reshape(bf16[4718592]{0:T(1024)(128)(2,1)} %slice.224) | data formatting | bytes 18874368 | tf_op jit(solution)/shard_map/slice | solution.py:54
  752.7 78.2 %while.34 = (s32[]{:T(128)}, f32[256,256]{1,0:T(8,128)S(1)}, f32[12,4,256]{2,1,0:T(4,128)S(1)}, f32[12,4,256]{2,1,0:T(4,128)S(1)}, f32[12,4,256,64]{2,3,1,0:T(8,...) while((s32[]{:T(128)}, f32[256,256]{1,0:T(8,128)S(1)}, ...), condition=%wide.region_12.13_spmd.clone, body=%wide.region_7.12_spmd.clone.sunk | while | flops 407370752 | bytes 4986067 | solution.py:109
  844.7 8.4 multiply_reduce_fusion.4
  857.8 6.8 pad_add_fusion
  864.6 12.9 fusion.72
  877.5 13.1 convolution_convert_fusion
  890.6 18.1 %convert_element_type.108 = bf16[4718592]{0:T(1024)(128)(2,1)} reshape(bf16[3072,1536]{1,0:T(8,128)(2,1)} %convolution_convert_fusion.1) | data formatting | bytes 18874368 | tf_op jit(solution)/shard_map/convert_element_type | solution.py:175
  909.7 25.0 %copy.31 = bf16[1536,6448]{1,0:T(8,128)(2,1)} copy(bf16[1536,6448]{0,1:T(8,128)(2,1)} %convolution_convert_fusion) | data formatting | bytes 39616512 | tf_op jit(solution)/shard_map/convert_element_type | solution.py:175
  934.8 36.0 %convert_element_type.106 = bf16[9904128]{0:T(1024)(128)(2,1)} reshape(bf16[1536,6448]{1,0:T(8,128)(2,1)} %copy.31) | data formatting | bytes 39616512 | tf_op jit(solution)/shard_map/convert_element_type | solution.py:175
  970.9 16.7 %dynamic_update_slice.61 = bf16[14647296]{0:T(1024)(128)(2,1)} pad(bf16[9904128]{0:T(1024)(128)(2,1)} %convert_element_type.106, bf16[]{:T(256)} %constant.169.clone.1), padding=0_4743168 | pad | bytes 49102848 | tf_op jit(solution)/shard_map/dynamic_update_slice | solution.py:176
  987.6 8.7 constant_dynamic-update-slice_fusion.1
  1010.5 8.6 fusion.68
  1019.1 431.9 %all-reduce.19.cloned.1.call-done = bf16[14647296]{0:T(1024)(128)(2,1)} async-done(((bf16[14647296]{0:T(1024)(128)(2,1)}), bf16[14647296]{0:T(1024)(128)(2,1)}) %all-reduce.19.cloned.1.call-update) | async-done | bytes 29294608 | tf_op jit(solution)/shard_map/psum | solution.py:178
  1451.0 90.1 %multiply_subtract_fusion = (f32[7323648]{0:T(1024)}, f32[7323648]{0:T(1024)}, f32[7323648]{0:T(1024)}) fusion(f32[7323648]{0:T(1024)} %param.15, f32[]{:T(128)} %bitcast.37, f32[]{:T(128)} %bitcast.36, f32[]{:T(128)} %bitcast.35, f32[]{:T(128)} %bitcast.34, f32[]{:T(128)} %bitcast.33, f32[]{:T(128)} %bitcast.32, f32[]{:T(128)} %bitcast.31, f32[]{:T(128)} %bitcast.30, ...), kind=kLoop, calls=%fused_computation.50 | loop fusion | flops 563920896 | bytes 190414928 | tf_op jit(solution)/shard_map/sub | solution.py:139
  (330 shorter events, 210.3 us)
Async XLA Ops:
  7.2 1443.8 %all-reduce.19.cloned.1.call-start = ((), (), s32[]{:S(2)}) async-start(), calls=%async_computation | async-start | bytes 58589184 | tf_op jit(solution)/shard_map/psum | solution.py:178
  24.6 23.3 %collective-permute-start = (bf16[457728]{0:T(1024)(128)(2,1)S(1)}, bf16[457728]{0:T(1024)(128)(2,1)S(1)}, u32[]{:S(2)}, u32[]{:S(2)}) collective-permute-start(bf16[457728]{0:T(1024)(128)(2,1)S(1)} %dynamic_slice.59), channel_id=1, source_target_pairs={{0,1},{1,0},{2,3},{3,2},{4,5},{5,4},{6,7},{7,6},{8,9},{9,8},{10,11... | collective-permute-start | bytes 2746376 | tf_op jit(solution)/shard_map/ppermute | solution.py:152
  59.1 4.0 collective-permute-start.1
  78.9 42.2 %collective-permute-start.2 = (bf16[2,457728]{1,0:T(2,128)(2,1)S(1)}, bf16[2,457728]{1,0:T(2,128)(2,1)}, u32[]{:S(2)}, u32[]{:S(2)}) collective-permute-start(bf16[2,457728]{1,0:T(2,128)(2,1)S(1)} %pad_maximum_fusion.3), channel_id=1, source_target_pairs={{0,4},{2,6},{4,0},{6,2},{8,12},{10,14},{12,8},{14,10},{16,20},{18,... | collective-permute-start | bytes 5492744 | tf_op jit(solution)/shard_map/ppermute | solution.py:32
  132.9 80.7 %collective-permute-start.3 = (bf16[4,457728]{1,0:T(4,128)(2,1)}, bf16[4,457728]{1,0:T(4,128)(2,1)}, u32[]{:S(2)}, u32[]{:S(2)}) collective-permute-start(bf16[4,457728]{1,0:T(4,128)(2,1)} %pad_maximum_fusion.2), channel_id=1, source_target_pairs={{0,8},{2,10},{4,12},{6,14},{8,0},{10,2},{12,4},{14,6},{16,24},{18,... | collective-permute-start | bytes 10985480 | tf_op jit(solution)/shard_map/ppermute | solution.py:32
  220.7 8.7 copy-start.15
  220.8 9.0 copy-start.22
  226.7 316.2 %collective-permute-start.4 = (bf16[8,457728]{1,0:T(8,128)(2,1)}, bf16[8,457728]{1,0:T(8,128)(2,1)}, u32[]{:S(2)}, u32[]{:S(2)}) collective-permute-start(bf16[8,457728]{1,0:T(8,128)(2,1)} %pad_maximum_fusion.1), channel_id=1, source_target_pairs={{0,16},{2,18},{4,20},{6,22},{8,24},{10,26},{12,28},{14,30},{16,0},... | collective-permute-start | bytes 21970952 | tf_op jit(solution)/shard_map/ppermute | solution.py:32
  229.7 321.4 %copy-start.37 = (f32[256]{0:T(256)}, f32[256]{0:T(256)S(1)}, u32[]{:S(2)}) copy-start(f32[256]{0:T(256)S(1)} %fusion.75) | copy-start | bytes 3076
  229.8 413.2 %copy-start.49 = (f32[256]{0:T(256)}, f32[256]{0:T(256)S(1)}, u32[]{:S(2)}) copy-start(f32[256]{0:T(256)S(1)} %fusion.99) | copy-start | bytes 3076
  229.8 426.4 %copy-start.39 = (pred[256]{0:T(512)(128)(4,1)}, pred[256]{0:T(512)(128)(4,1)S(1)}, u32[]{:S(2)}) copy-start(pred[256]{0:T(512)(128)(4,1)S(1)} %get-tuple-element.470) | copy-start | bytes 772
  229.8 426.4 %copy-start.41 = (pred[256]{0:T(512)(128)(4,1)}, pred[256]{0:T(512)(128)(4,1)S(1)}, u32[]{:S(2)}) copy-start(pred[256]{0:T(512)(128)(4,1)S(1)} %get-tuple-element.471) | copy-start | bytes 772
  229.8 426.4 %copy-start.43 = (pred[256]{0:T(512)(128)(4,1)}, pred[256]{0:T(512)(128)(4,1)S(1)}, u32[]{:S(2)}) copy-start(pred[256]{0:T(512)(128)(4,1)S(1)} %get-tuple-element.472) | copy-start | bytes 772
  589.9 66.4 %copy-start.25 = (f32[3328]{0:T(1024)}, f32[3328]{0:T(1024)S(1)}, u32[]{:S(2)}) copy-start(f32[3328]{0:T(1024)S(1)} %get-tuple-element.448) | copy-start | bytes 39940
  589.9 66.4 %copy-start.27 = (f32[3328]{0:T(1024)}, f32[3328]{0:T(1024)S(1)}, u32[]{:S(2)}) copy-start(f32[3328]{0:T(1024)S(1)} %get-tuple-element.449) | copy-start | bytes 39940
  589.9 66.4 %copy-start.29 = (f32[3328]{0:T(1024)}, f32[3328]{0:T(1024)S(1)}, u32[]{:S(2)}) copy-start(f32[3328]{0:T(1024)S(1)} %get-tuple-element.450) | copy-start | bytes 39940
  589.9 66.4 %copy-start.31 = (f32[3328]{0:T(1024)}, f32[3328]{0:T(1024)S(1)}, u32[]{:S(2)}) copy-start(f32[3328]{0:T(1024)S(1)} %get-tuple-element.451) | copy-start | bytes 39940
  656.0 20.7 %copy-start.9 = (f32[256,6448]{0,1:T(8,128)}, f32[256,6448]{0,1:T(8,128)S(1)}, u32[]{:S(2)}) copy-start(f32[256,6448]{0,1:T(8,128)S(1)} %fusion.80) | copy-start | bytes 19808260
  656.3 7.9 copy-start.5
  667.6 9.1 copy-start.46
  667.6 9.1 copy-start.52
  678.2 30.3 %copy-start.48 = (f32[48]{0:T(128)S(1)}, f32[48]{0:T(128)}, u32[]{:S(2)}) copy-start(f32[48]{0:T(128)} %get-tuple-element.430) | copy-start | bytes 580
  744.0 8.8 copy-start.14
  844.7 8.4 copy-start.26
  844.7 8.4 copy-start.28
  844.7 8.4 copy-start.30
  844.7 8.4 copy-start.32
  857.8 6.8 copy-start.50
  890.6 18.1 %copy-start.35 = (f32[3072]{0:T(1024)S(1)}, f32[3072]{0:T(1024)}, u32[]{:S(2)}) copy-start(f32[3072]{0:T(1024)} %get-tuple-element.413) | copy-start | bytes 36868
  890.6 19.0 %copy-start.34 = (f32[3328]{0:T(1024)S(1)}, f32[3328]{0:T(1024)}, u32[]{:S(2)}) copy-start(f32[3328]{0:T(1024)} %get-tuple-element.365) | copy-start | bytes 39940
  987.5 9.3 copy-start.36
  987.5 12.2 copy-start.45
  (39 other events, 174.9 us)
Sparse Core Ops, SparseCore 0:
  1005.9 445.0 all-reduce.18
